TPU v7x, 512 devices: a whole 4x8x8 slice. The times are simulated.
512 devices in a mesh: row: 32 (over x, z), col: 16 (over y, core).
Axes of the slice: x: 4, y: 8, z: 8, core: 2. Of those that a mesh axis runs over, the one named last changes fastest.
Arguments:
- matrix: float32 [14336, 14336], P('row', 'col'), may hold values from -3 to 3
- reflectors: float32 [1, 64, 14336], P(None, None, 'row'), may hold values from -0.09375 to 0.09375
- factors: float32 [1, 64, 64], replicated, may hold values from -0.1 to 2, as said below
Outputs:
- updated: float32 [14336, 14336], P('row', 'col')
- companions: float32 [1, 64, 14336], P(None, None, 'row')
Inputs may be any that keep to these rules, and one draw needn't show every extreme that they name: `factors`: each factor is upper triangular (zero below the diagonal) with diagonal entries between 1 and 2.
All inputs are finite; a program needn't handle non-finite values.
Results may differ from a plain program's by a relative error of at most 0.0001.
Values sent between devices are 32-bit elements; how exact they have to be, the bound alone decides.
No kernel may reach another device: no remote copies, remote signals or barrier semaphores. Data moves between devices by JAX's collectives and lax.ppermute only.
A program may use at most 64 MiB of HBM per device.

v0:
```python
import jax
import jax.numpy as jnp
from jax import lax
from jax.sharding import Mesh
from jax.sharding import PartitionSpec as P


def contract(left_side, right_side, left_dim, right_dim):
    return lax.dot_general(
        left_side,
        right_side,
        (((left_dim,), (right_dim,)), ((), ())),
        precision=lax.Precision.HIGHEST,
        preferred_element_type=jnp.float32,
    )


def gathered_sum(values, axes):
    for axis in axes:
        values = jnp.sum(lax.all_gather(values, axis), axis=0)
    return values


def split_sum(values, axis, split_axis):
    width = values.shape[1] // 2
    mine = jnp.where(lax.axis_index(split_axis) == 0, values[:, :width], values[:, width:])
    total = gathered_sum(mine, (axis,))
    both = lax.all_gather(total, split_axis)
    return jnp.concatenate([both[0], both[1]], axis=1)


def scattered_sum(values, axis, parts):
    chunks = values.reshape((parts, values.shape[0] // parts) + values.shape[1:])
    mine = jnp.sum(lax.all_to_all(chunks, axis, 0, 0, tiled=False), axis=0)
    return lax.all_gather(mine, axis, tiled=True)


def scattered_sum_nested(values, axes, inner_axes=()):
    if not axes:
        return gathered_sum(values, inner_axes)
    parts = lax.axis_size(axes[0])
    chunks = values.reshape((parts, values.shape[0] // parts) + values.shape[1:])
    mine = jnp.sum(lax.all_to_all(chunks, axes[0], 0, 0, tiled=False), axis=0)
    mine = scattered_sum_nested(mine, axes[1:], inner_axes)
    return lax.all_gather(mine, axes[0], tiled=True)


def halves_sum(values, axis):
    width = values.shape[1] // 2
    left = gathered_sum(values[:, :width], (axis,))
    right = gathered_sum(values[:, width:], (axis,))
    return jnp.concatenate([left, right], axis=1)


def column_block_pairs(rows, cols, shift):
    group = rows // cols
    pairs = []
    for r in range(rows):
        for c in range(cols):
            target_row = group * c + (r % group - shift) % group
            pairs.append((r * cols + c, target_row * cols + r // group))
    return pairs


def staged_route(rows, cols):
    sizes = (4, rows // 4, cols // 2, 2)
    if rows % 4 or cols % 2 or sizes[2] % sizes[0]:
        return None
    k = sizes[2] // sizes[0]

    def split(i):
        return (
            i // (sizes[1] * sizes[2] * 2),
            i // (sizes[2] * 2) % sizes[1],
            i // 2 % sizes[2],
            i % 2,
        )

    def join(x, z, y, core):
        return ((x * sizes[1] + z) * sizes[2] + y) * 2 + core

    def hop(i):
        x, z, y, core = split(i)
        return join(y // k, z, k * x + y % k, core)

    return [(i, hop(i)) for i in range(rows * cols)]


def to_column_blocks(values, rows, cols, all_axes, row_index):
    group = rows // cols
    first = staged_route(rows, cols)
    if first is None:
        rounds = [
            lax.ppermute(values, all_axes, column_block_pairs(rows, cols, shift))
            for shift in range(group)
        ]
    else:
        moved = lax.ppermute(values, all_axes, first)
        rounds = []
        for shift in range(group):
            final = dict(column_block_pairs(rows, cols, shift))
            rounds.append(lax.ppermute(moved, all_axes, [(mid, final[i]) for i, mid in first]))
    offset = row_index % group
    blocks = []
    for part in range(group):
        block = rounds[0]
        for shift in range(1, group):
            block = jnp.where((part - offset) % group == shift, rounds[shift], block)
        blocks.append(block)
    return jnp.concatenate(blocks, axis=values.ndim - 1)


def second_hops(moved, rows, cols, all_axes, row_index):
    group = rows // cols
    first = staged_route(rows, cols)
    rounds = []
    for shift in range(group):
        final = dict(column_block_pairs(rows, cols, shift))
        rounds.append(lax.ppermute(moved, all_axes, [(mid, final[i]) for i, mid in first]))
    offset = row_index % group
    blocks = []
    for part in range(group):
        block = rounds[0]
        for shift in range(1, group):
            block = jnp.where((part - offset) % group == shift, rounds[shift], block)
        blocks.append(block)
    return jnp.concatenate(blocks, axis=moved.ndim - 1)


def make_shards(row_axes, col_axes, rows, cols):
    all_axes = tuple(row_axes) + tuple(col_axes)

    def shards(matrix, reflectors, factors):
        current = matrix
        v_rows = reflectors[0]
        factor = factors[0]
        row_index = lax.axis_index(tuple(row_axes))
        chunks = contract(v_rows, current, 1, 0)
        first = row_axes[-1]
        parts = lax.axis_size(first)
        chunks = chunks.reshape((parts, chunks.shape[0] // parts) + chunks.shape[1:])
        mine = jnp.sum(lax.all_to_all(chunks, first, 0, 0, tiled=False), axis=0)
        mine, v_sent = lax.optimization_barrier((mine, v_rows))
        moved = lax.ppermute(v_sent, all_axes, staged_route(rows, cols))
        second = row_axes[-2]
        parts2 = lax.axis_size(second)
        chunks = mine.reshape((parts2, mine.shape[0] // parts2) + mine.shape[1:])
        mine = jnp.sum(lax.all_to_all(chunks, second, 0, 0, tiled=False), axis=0)
        mine = gathered_sum(mine, row_axes[:1])
        mine, moved = lax.optimization_barrier((mine, moved))
        v_cols = second_hops(moved, rows, cols, all_axes, row_index)
        mine = lax.all_gather(mine, second, tiled=True)
        col_sums = lax.all_gather(mine, first, tiled=True)
        partial_value = contract(v_cols, current, 1, 1)
        partial_inner = contract(v_cols, col_sums, 1, 1)
        width = partial_value.shape[1]
        sums = split_sum(
            gathered_sum(jnp.concatenate([partial_value, partial_inner], axis=1), col_axes[1:]),
            col_axes[0],
            col_axes[1],
        )
        row_sums = sums[:, :width]
        inner = sums[:, width:]
        x_rows = contract(factor, row_sums, 0, 0)
        x_cols = contract(factor, col_sums, 0, 0)
        projected = contract(inner, factor, 0, 0)
        mixing = contract(projected, factor, 0, 0)
        w_rows = x_rows - 0.5 * contract(mixing, v_rows, 1, 0)
        w_cols = x_cols - 0.5 * contract(mixing, v_cols, 1, 0)
        current = current - contract(
            jnp.concatenate([v_rows, w_rows], axis=0),
            jnp.concatenate([w_cols, v_cols], axis=0),
            0,
            0,
        )
        return (current, jnp.stack([w_rows]))

    return shards


def solution(mesh):
    rows, cols = (mesh.shape["row"], mesh.shape["col"])
    row_axes, col_axes = (("x", "za", "zb"), ("y", "core"))
    fine = Mesh(mesh.devices.reshape((4, rows // 8, 2, cols // 2, 2)), row_axes + col_axes)
    return jax.shard_map(
        make_shards(row_axes, col_axes, rows, cols),
        mesh=fine,
        in_specs=(P(row_axes, col_axes), P(None, None, row_axes), P()),
        out_specs=(P(row_axes, col_axes), P(None, None, row_axes)),
        check_vma=False,
    )
```

profile of v0, /device:TPU:1, one launch (start us, length us, event | category | flops | bytes accessed | tf_op | source)
XLA Modules:
  0.0 111.3 jit_solution(5235569078798116109)
XLA Ops:
  0.6 0.0 copy-start
  0.6 0.0 copy-start.2
  0.7 2.6 %fusion = f32[2,32,896]{2,1,0:T(8,128)S(1)} fusion(f32[2,32,448]{2,1,0:T(8,128)} %bitcast.36, f32[448,896]{1,0:T(8,128)} %param.3), kind=kOutput, calls=%fused_computation | convolution fusion | flops 308281344 | bytes 1949696 | tf_op jit(solution)/shard_map/dot_general | solution.py:9
  3.2 7.8 %all_to_all.10 = f32[2,32,896]{2,1,0:T(8,128)S(1)} all-to-all(f32[2,32,896]{2,1,0:T(8,128)S(1)} %fusion), channel_id=1, replica_groups=mesh['x'=4,'za'=4,'zb'=2,'y'=8,'core'=2] {'zb'}, dimensions={0} | all-to-all | bytes 458752 | tf_op jit(solution)/shard_map/all_to_all | solution.py:142
  11.1 0.7 reduce_sum.45
  11.7 9.2 %all-to-all-start.1 = ((f32[4,8,896]{2,1,0:T(8,128)}), f32[4,8,896]{2,1,0:T(8,128)S(1)}, u32[]{:S(2)}, u32[]{:S(2)}) async-start(f32[4,8,896]{2,1,0:T(8,128)} %bitcast.3), calls=%async_computation.1 | async-start | bytes 229376 | tf_op jit(solution)/shard_map/all_to_all | solution.py:148
  20.9 0.0 copy-done.2
  20.9 0.7 collective-permute-start
  21.6 6.5 %all-to-all-done.1 = f32[4,8,896]{2,1,0:T(8,128)S(1)} async-done(((f32[4,8,896]{2,1,0:T(8,128)}), f32[4,8,896]{2,1,0:T(8,128)S(1)}, u32[]{:S(2)}, u32[]{:S(2)}) %all-to-all-start.1) | async-done | bytes 114720 | tf_op jit(solution)/shard_map/all_to_all | solution.py:148
  28.1 10.1 %all-gather = f32[32,896]{1,0:T(8,128)S(1)} all-gather(f32[8,896]{1,0:T(8,128)S(1)} %reduce_sum.46), channel_id=2, replica_groups=mesh['x'=4,'za'=4,'zb'=2,'y'=8,'core'=2] {'x'}, dimensions={0}, use_global_device_ids=true | all-gather | bytes 143360 | tf_op jit(solution)/shard_map/all_gather | solution.py:20
  38.2 0.0 collective-permute-done
  38.2 9.6 %collective-permute-start.2 = (f32[64,448]{1,0:T(8,128)S(1)}, f32[64,448]{1,0:T(8,128)S(1)}, u32[]{:S(2)}, u32[]{:S(2)}) collective-permute-start(f32[64,448]{1,0:T(8,128)S(1)} %collective-permute-done), channel_id=1, source_target_pairs={{0,0},{1,32},{2,64},{3,96},{128,128},{129,160},{130,192},{131,224}... | collective-permute-start | bytes 344072 | tf_op jit(solution)/shard_map/ppermute | solution.py:119
  47.8 1.9 %collective-permute-start.1 = (f32[64,448]{1,0:T(8,128)S(1)}, f32[64,448]{1,0:T(8,128)S(1)}, u32[]{:S(2)}, u32[]{:S(2)}) collective-permute-start(f32[64,448]{1,0:T(8,128)S(1)} %collective-permute-done), channel_id=1, source_target_pairs={{0,16},{1,48},{2,80},{3,112},{128,144},{129,176},{130,208},{131,24... | collective-permute-start | bytes 344072 | tf_op jit(solution)/shard_map/ppermute | solution.py:119
  49.7 17.0 %all_gather.32 = f32[32,896]{1,0:T(8,128)S(1)} all-gather(f32[8,896]{1,0:T(8,128)S(1)} %bitcast_reduce_fusion), channel_id=1, replica_groups=mesh['x'=4,'za'=4,'zb'=2,'y'=8,'core'=2] {'za'}, dimensions={0}, use_global_device_ids=true | all-gather | bytes 143360 | tf_op jit(solution)/shard_map/all_gather | solution.py:152
  66.8 4.3 %all_gather.33 = f32[64,896]{1,0:T(8,128)S(1)} all-gather(f32[32,896]{1,0:T(8,128)S(1)} %all_gather.32), channel_id=1, replica_groups=mesh['x'=4,'za'=4,'zb'=2,'y'=8,'core'=2] {'zb'}, dimensions={0}, use_global_device_ids=true | all-gather | bytes 344064 | tf_op jit(solution)/shard_map/all_gather | solution.py:153
  71.1 0.0 copy-done
  71.1 0.4 convolution_bitcast_fusion
  71.5 0.0 collective-permute-done.2
  71.5 0.0 collective-permute-done.1
  71.5 0.4 fusion.13
  71.9 1.7 %fusion.14 = f32[64,448]{1,0:T(8,128)S(1)} fusion(f32[448,896]{1,0:T(8,128)S(1)} %copy-done.1, f32[64,448]{1,0:T(8,128)S(1)} %get-tuple-element.11, f32[64,448]{1,0:T(8,128)S(1)} %get-tuple-element.10), kind=kOutput, calls=%fused_computation.22 | convolution fusion | flops 308338688 | bytes 1949696 | tf_op jit(solution)/shard_map/dot_general | solution.py:9
  73.6 0.1 pad_maximum_fusion.3
  73.7 5.9 %all-gather.1 = f32[128,512]{1,0:T(8,128)S(1)} all-gather(f32[64,512]{1,0:T(8,128)S(1)} %pad_maximum_fusion.3), channel_id=3, replica_groups=mesh['x'=4,'za'=4,'zb'=2,'y'=8,'core'=2] {'core'}, dimensions={0}, use_global_device_ids=true | all-gather | bytes 393216 | tf_op jit(solution)/shard_map/all_gather | solution.py:20
  79.6 19.5 %all-gather.2 = f32[512,256]{1,0:T(8,128)S(1)} all-gather(f32[64,256]{1,0:T(8,128)S(1)} %slice_select_fusion), channel_id=4, replica_groups=mesh['x'=4,'za'=4,'zb'=2,'y'=8,'core'=2] {'y'}, dimensions={0}, use_global_device_ids=true | all-gather | bytes 589824 | tf_op jit(solution)/shard_map/all_gather | solution.py:20
  99.2 7.9 %all-gather.3 = f32[128,256]{1,0:T(8,128)S(1)} all-gather(f32[64,256]{1,0:T(8,128)S(1)} %reduce_sum.49), channel_id=5, replica_groups=mesh['x'=4,'za'=4,'zb'=2,'y'=8,'core'=2] {'core'}, dimensions={0}, use_global_device_ids=true | all-gather | bytes 196608 | tf_op jit(solution)/shard_map/all_gather | solution.py:28
  107.1 0.3 fusion.15
  107.4 0.2 fusion.18
  107.7 0.3 convolution_multiply_fusion.1
  107.9 0.4 fusion.2
  108.3 0.3 fusion.3
  108.7 0.0 copy-start.3
  108.7 2.6 %convolution_subtract_fusion = f32[448,896]{1,0:T(8,128)} fusion(f32[448,896]{1,0:T(8,128)S(1)} %copy-done.1, f32[64,448]{1,0:T(8,128)S(1)} %get-tuple-element.11, f32[64,448]{1,0:T(8,128)S(1)} %get-tuple-element.10, f32[64,896]{1,0:T(8,128)S(1)} %fusion.2, f32[64,448]{1,0:T(8,128)S(1)} %fusion.3, f32[64,448]{1,0:T(8,128)S(1)} %bitcast.38), kind=kOutput, calls=%fused_computation.2 | convolution fusion | flops 617250816 | bytes 3899392 | tf_op jit(solution)/shard_map/dot_general | solution.py:9
  (10 shorter events, 0.1 us)
Async XLA Ops:
  0.6 70.4 %copy-start = (f32[1,64,64]{2,1,0:T(8,128)S(1)}, f32[1,64,64]{2,1,0:T(8,128)}, u32[]{:S(2)}) copy-start(f32[1,64,64]{2,1,0:T(8,128)} %param.5) | copy-start | bytes 49156
  0.6 20.3 %copy-start.2 = (f32[1,64,448]{2,1,0:T(8,128)S(1)}, f32[1,64,448]{2,1,0:T(8,128)}, u32[]{:S(2)}) copy-start(f32[1,64,448]{2,1,0:T(8,128)} %param.4) | copy-start | bytes 344068
  11.1 60.9 %copy-start.1 = (f32[448,896]{1,0:T(8,128)S(1)}, f32[448,896]{1,0:T(8,128)}, u32[]{:S(2)}) copy-start(f32[448,896]{1,0:T(8,128)} %param.3) | copy-start | bytes 4816900
  11.7 16.4 %all-to-all-start.1 = ((f32[4,8,896]{2,1,0:T(8,128)}), f32[4,8,896]{2,1,0:T(8,128)S(1)}, u32[]{:S(2)}, u32[]{:S(2)}) async-start(f32[4,8,896]{2,1,0:T(8,128)} %bitcast.3), calls=%async_computation.1 | async-start | bytes 229376 | tf_op jit(solution)/shard_map/all_to_all | solution.py:148
  20.9 17.3 %collective-permute-start = (f32[64,448]{1,0:T(8,128)S(1)}, f32[64,448]{1,0:T(8,128)S(1)}, u32[]{:S(2)}, u32[]{:S(2)}) collective-permute-start(f32[64,448]{1,0:T(8,128)S(1)} %bitcast.37), channel_id=1, source_target_pairs={{0,0},{1,1},{2,2},{3,3},{4,128},{5,129},{6,130},{7,131},{8,256},{9... | collective-permute-start | bytes 344072 | tf_op jit(solution)/shard_map/ppermute | solution.py:144
  38.2 33.2 %collective-permute-start.2 = (f32[64,448]{1,0:T(8,128)S(1)}, f32[64,448]{1,0:T(8,128)S(1)}, u32[]{:S(2)}, u32[]{:S(2)}) collective-permute-start(f32[64,448]{1,0:T(8,128)S(1)} %collective-permute-done), channel_id=1, source_target_pairs={{0,0},{1,32},{2,64},{3,96},{128,128},{129,160},{130,192},{131,224}... | collective-permute-start | bytes 344072 | tf_op jit(solution)/shard_map/ppermute | solution.py:119
  47.8 23.7 %collective-permute-start.1 = (f32[64,448]{1,0:T(8,128)S(1)}, f32[64,448]{1,0:T(8,128)S(1)}, u32[]{:S(2)}, u32[]{:S(2)}) collective-permute-start(f32[64,448]{1,0:T(8,128)S(1)} %collective-permute-done), channel_id=1, source_target_pairs={{0,16},{1,48},{2,80},{3,112},{128,144},{129,176},{130,208},{131,24... | collective-permute-start | bytes 344072 | tf_op jit(solution)/shard_map/ppermute | solution.py:119
  108.7 2.7 %copy-start.3 = (f32[64,448]{1,0:T(8,128)}, f32[64,448]{1,0:T(8,128)S(1)}, u32[]{:S(2)}) copy-start(f32[64,448]{1,0:T(8,128)S(1)} %fusion.3) | copy-start | bytes 344068
where the time goes:
time: 112 us; the launch traced here: 111 us
  blocking collectives  72.6 us (65%)
  starting transfers between devices  21.4 us (19%)
  matrix products  9.15 us (8%)
  waiting for transfers between devices  6.48 us (6%)
    all_gather x3, blocking collectives, gathered_sum(): values = jnp.sum(lax.all_gather(values, axis), axis=0)  35.6 us
    all_gather x1, blocking collectives, shards(): mine = lax.all_gather(mine, second, tiled=True)  17 us
    ppermute x2, starting transfers between devices, second_hops(): lax.ppermute(moved, all_axes, [(mid, final[i]) for i, mid in first])  11.5 us
    all_to_all x1, starting transfers between devices, shards(): mine = jnp.sum(lax.all_to_all(chunks, second, 0, 0, tiled=False), axis=0)  9.22 us
    dot_general x10, matrix products, contract(): lax.dot_general(left_side, right_side, (((left_dim,), (right_dim,)), ((),...  9.15 us
    all_gather x1, blocking collectives, split_sum(): both = lax.all_gather(total, split_axis)  7.91 us
    all_to_all x1, blocking collectives, shards(): mine = jnp.sum(lax.all_to_all(chunks, first, 0, 0, tiled=False), axis=0)  7.84 us
    all_to_all x1, waiting for transfers between devices, shards(): mine = jnp.sum(lax.all_to_all(chunks, second, 0, 0, tiled=False), axis=0)  6.47 us
  transfers between devices with their start and end apart: 4, of which 1 were waited for; matrix products, arithmetic and copies ran while one was open for 0% of the time, Pallas kernels for 0%

commit v1 on v0

--- a/solution.py
+++ b/solution.py
@@ -150,7 +150,9 @@
         mine, moved = lax.optimization_barrier((mine, moved))
         v_cols = second_hops(moved, rows, cols, all_axes, row_index)
         mine = lax.all_gather(mine, second, tiled=True)
-        col_sums = lax.all_gather(mine, first, tiled=True)
+        col_sums = jnp.concatenate(
+            lax.all_to_all(jnp.stack([mine] * lax.axis_size(first)), first, 0, 0), axis=0
+        )
         partial_value = contract(v_cols, current, 1, 1)
         partial_inner = contract(v_cols, col_sums, 1, 1)
         width = partial_value.shape[1]

time: 112 us -> 114 us (1.018)
  blocking collectives: 72.6 us -> 68.5 us
  starting transfers between devices: 21.4 us -> 24.8 us
  waiting for transfers between devices: 6.48 us -> 8.6 us
    all_gather x1 -> x0, blocking collectives: 4.31 us -> none  [shards(): col_sums = lax.all_gather(mine, first, tiled=True)]
    all_to_all x0 -> x1, starting transfers between devices: none -> 3.44 us  [shards(): lax.all_to_all(jnp.stack([mine] * lax.axis_size(first)), first, 0, 0)]
    all_to_all x0 -> x1, waiting for transfers between devices: none -> 2.12 us  [shards(): lax.all_to_all(jnp.stack([mine] * lax.axis_size(first)), first, 0, 0)]
  transfers between devices with their start and end apart: 4 -> 5, of which waited for: 1 -> 2; matrix products, arithmetic and copies ran while one was open for 0% -> 2% of each run, Pallas kernels for 0% -> 0%
where the time goes in v1:
time: 114 us; the launch traced here: 113 us
  blocking collectives  68.5 us (60%)
  starting transfers between devices  24.8 us (22%)
  matrix products  9.15 us (8%)
  waiting for transfers between devices  8.6 us (8%)
  other arithmetic  1.55 us (1%)
    all_gather x3, blocking collectives, gathered_sum(): values = jnp.sum(lax.all_gather(values, axis), axis=0)  35.6 us
    all_gather x1, blocking collectives, shards(): mine = lax.all_gather(mine, second, tiled=True)  17 us
    ppermute x2, starting transfers between devices, second_hops(): lax.ppermute(moved, all_axes, [(mid, final[i]) for i, mid in first])  11.5 us
    all_to_all x1, starting transfers between devices, shards(): mine = jnp.sum(lax.all_to_all(chunks, second, 0, 0, tiled=False), axis=0)  9.22 us
    dot_general x10, matrix products, contract(): lax.dot_general(left_side, right_side, (((left_dim,), (right_dim,)), ((),...  9.15 us
    all_to_all x1, blocking collectives, shards(): mine = jnp.sum(lax.all_to_all(chunks, first, 0, 0, tiled=False), axis=0)  7.97 us
    all_gather x1, blocking collectives, split_sum(): both = lax.all_gather(total, split_axis)  7.92 us
    all_to_all x1, waiting for transfers between devices, shards(): mine = jnp.sum(lax.all_to_all(chunks, second, 0, 0, tiled=False), axis=0)  6.47 us
  transfers between devices with their start and end apart: 5, of which 2 were waited for; matrix products, arithmetic and copies ran while one was open for 2% of the time, Pallas kernels for 0%

profile of v1, /device:TPU:1, one launch (start us, length us, event | category | flops | bytes accessed | tf_op | source)
XLA Modules:
  0.0 113.4 jit_solution(12588668893226015279)
XLA Ops:
  0.6 0.0 copy-start
  0.7 2.6 %fusion = f32[2,32,896]{2,1,0:T(8,128)S(1)} fusion(f32[2,32,448]{2,1,0:T(8,128)} %bitcast.40, f32[448,896]{1,0:T(8,128)} %param.3), kind=kOutput, calls=%fused_computation | convolution fusion | flops 308281344 | bytes 1949696 | tf_op jit(solution)/shard_map/dot_general | solution.py:9
  3.2 0.0 copy-start.1
  3.2 8.0 %all_to_all.15 = f32[2,32,896]{2,1,0:T(8,128)S(1)} all-to-all(f32[2,32,896]{2,1,0:T(8,128)S(1)} %fusion), channel_id=1, replica_groups=mesh['x'=4,'za'=4,'zb'=2,'y'=8,'core'=2] {'zb'}, dimensions={0} | all-to-all | bytes 458752 | tf_op jit(solution)/shard_map/all_to_all | solution.py:142
  11.2 0.7 reduce_sum.45
  11.9 9.2 %all-to-all-start.1 = ((f32[4,8,896]{2,1,0:T(8,128)}), f32[4,8,896]{2,1,0:T(8,128)S(1)}, u32[]{:S(2)}, u32[]{:S(2)}) async-start(f32[4,8,896]{2,1,0:T(8,128)} %bitcast.3), calls=%async_computation.1 | async-start | bytes 229376 | tf_op jit(solution)/shard_map/all_to_all | solution.py:148
  21.1 0.7 collective-permute-start
  21.8 6.5 %all-to-all-done.1 = f32[4,8,896]{2,1,0:T(8,128)S(1)} async-done(((f32[4,8,896]{2,1,0:T(8,128)}), f32[4,8,896]{2,1,0:T(8,128)S(1)}, u32[]{:S(2)}, u32[]{:S(2)}) %all-to-all-start.1) | async-done | bytes 114720 | tf_op jit(solution)/shard_map/all_to_all | solution.py:148
  28.2 10.1 %all-gather = f32[32,896]{1,0:T(8,128)S(1)} all-gather(f32[8,896]{1,0:T(8,128)S(1)} %reduce_sum.46), channel_id=2, replica_groups=mesh['x'=4,'za'=4,'zb'=2,'y'=8,'core'=2] {'x'}, dimensions={0}, use_global_device_ids=true | all-gather | bytes 143360 | tf_op jit(solution)/shard_map/all_gather | solution.py:20
  38.4 0.0 collective-permute-done
  38.4 9.6 %collective-permute-start.2 = (f32[64,448]{1,0:T(8,128)S(1)}, f32[64,448]{1,0:T(8,128)S(1)}, u32[]{:S(2)}, u32[]{:S(2)}) collective-permute-start(f32[64,448]{1,0:T(8,128)S(1)} %collective-permute-done), channel_id=1, source_target_pairs={{0,0},{1,32},{2,64},{3,96},{128,128},{129,160},{130,192},{131,224}... | collective-permute-start | bytes 344072 | tf_op jit(solution)/shard_map/ppermute | solution.py:119
  48.0 1.9 %collective-permute-start.1 = (f32[64,448]{1,0:T(8,128)S(1)}, f32[64,448]{1,0:T(8,128)S(1)}, u32[]{:S(2)}, u32[]{:S(2)}) collective-permute-start(f32[64,448]{1,0:T(8,128)S(1)} %collective-permute-done), channel_id=1, source_target_pairs={{0,16},{1,48},{2,80},{3,112},{128,144},{129,176},{130,208},{131,24... | collective-permute-start | bytes 344072 | tf_op jit(solution)/shard_map/ppermute | solution.py:119
  49.9 17.0 %all_gather.29 = f32[32,896]{1,0:T(8,128)S(1)} all-gather(f32[8,896]{1,0:T(8,128)S(1)} %bitcast_reduce_fusion), channel_id=1, replica_groups=mesh['x'=4,'za'=4,'zb'=2,'y'=8,'core'=2] {'za'}, dimensions={0}, use_global_device_ids=true | all-gather | bytes 143360 | tf_op jit(solution)/shard_map/all_gather | solution.py:152
  66.9 0.7 pad_maximum_fusion.1
  67.6 3.4 %all-to-all-start.2 = ((f32[2,32,896]{2,1,0:T(8,128)}), f32[2,32,896]{2,1,0:T(8,128)S(1)}, u32[]{:S(2)}, u32[]{:S(2)}) async-start(f32[2,32,896]{2,1,0:T(8,128)} %pad_maximum_fusion.1), calls=%async_computation.2 | async-start | bytes 458752 | tf_op jit(solution)/shard_map/all_to_all | solution.py:154
  71.0 0.0 collective-permute-done.2
  71.1 0.0 collective-permute-done.1
  71.1 1.7 %fusion.14 = f32[64,448]{1,0:T(8,128)S(1)} fusion(f32[448,896]{1,0:T(8,128)S(1)} %copy-done.1, f32[64,448]{1,0:T(8,128)S(1)} %get-tuple-element.11, f32[64,448]{1,0:T(8,128)S(1)} %get-tuple-element.10), kind=kOutput, calls=%fused_computation.23 | convolution fusion | flops 308338688 | bytes 1949696 | tf_op jit(solution)/shard_map/dot_general | solution.py:9
  72.8 2.1 %all-to-all-done.2 = f32[2,32,896]{2,1,0:T(8,128)S(1)} async-done(((f32[2,32,896]{2,1,0:T(8,128)}), f32[2,32,896]{2,1,0:T(8,128)S(1)}, u32[]{:S(2)}, u32[]{:S(2)}) %all-to-all-start.2) | async-done | bytes 229408 | tf_op jit(solution)/shard_map/all_to_all | solution.py:154
  74.9 0.4 fusion.13
  75.3 0.4 convolution_bitcast_fusion
  75.7 0.1 pad_maximum_fusion.4
  75.8 5.9 %all-gather.1 = f32[128,512]{1,0:T(8,128)S(1)} all-gather(f32[64,512]{1,0:T(8,128)S(1)} %pad_maximum_fusion.4), channel_id=3, replica_groups=mesh['x'=4,'za'=4,'zb'=2,'y'=8,'core'=2] {'core'}, dimensions={0}, use_global_device_ids=true | all-gather | bytes 393216 | tf_op jit(solution)/shard_map/all_gather | solution.py:20
  81.7 19.5 %all-gather.2 = f32[512,256]{1,0:T(8,128)S(1)} all-gather(f32[64,256]{1,0:T(8,128)S(1)} %slice_select_fusion), channel_id=4, replica_groups=mesh['x'=4,'za'=4,'zb'=2,'y'=8,'core'=2] {'y'}, dimensions={0}, use_global_device_ids=true | all-gather | bytes 589824 | tf_op jit(solution)/shard_map/all_gather | solution.py:20
  101.3 7.9 %all-gather.3 = f32[128,256]{1,0:T(8,128)S(1)} all-gather(f32[64,256]{1,0:T(8,128)S(1)} %reduce_sum.49), channel_id=5, replica_groups=mesh['x'=4,'za'=4,'zb'=2,'y'=8,'core'=2] {'core'}, dimensions={0}, use_global_device_ids=true | all-gather | bytes 196608 | tf_op jit(solution)/shard_map/all_gather | solution.py:28
  109.2 0.3 fusion.15
  109.5 0.2 fusion.18
  109.8 0.3 convolution_multiply_fusion.1
  110.0 0.4 fusion.2
  110.4 0.3 fusion.3
  110.8 0.0 copy-start.3
  110.8 2.6 %convolution_subtract_fusion = f32[448,896]{1,0:T(8,128)} fusion(f32[448,896]{1,0:T(8,128)S(1)} %copy-done.1, f32[64,448]{1,0:T(8,128)S(1)} %get-tuple-element.11, f32[64,448]{1,0:T(8,128)S(1)} %get-tuple-element.10, f32[64,896]{1,0:T(8,128)S(1)} %fusion.2, f32[64,448]{1,0:T(8,128)S(1)} %fusion.3, f32[64,448]{1,0:T(8,128)S(1)} %bitcast.42), kind=kOutput, calls=%fused_computation.2 | convolution fusion | flops 617250816 | bytes 3899392 | tf_op jit(solution)/shard_map/dot_general | solution.py:9
  (12 shorter events, 0.1 us)
Async XLA Ops:
  0.6 74.7 %copy-start = (f32[1,64,64]{2,1,0:T(8,128)S(1)}, f32[1,64,64]{2,1,0:T(8,128)}, u32[]{:S(2)}) copy-start(f32[1,64,64]{2,1,0:T(8,128)} %param.5) | copy-start | bytes 49156
  0.6 20.4 %copy-start.2 = (f32[1,64,448]{2,1,0:T(8,128)S(1)}, f32[1,64,448]{2,1,0:T(8,128)}, u32[]{:S(2)}) copy-start(f32[1,64,448]{2,1,0:T(8,128)} %param.4) | copy-start | bytes 344068
  3.2 67.9 %copy-start.1 = (f32[448,896]{1,0:T(8,128)S(1)}, f32[448,896]{1,0:T(8,128)}, u32[]{:S(2)}) copy-start(f32[448,896]{1,0:T(8,128)} %param.3) | copy-start | bytes 4816900
  11.9 16.4 %all-to-all-start.1 = ((f32[4,8,896]{2,1,0:T(8,128)}), f32[4,8,896]{2,1,0:T(8,128)S(1)}, u32[]{:S(2)}, u32[]{:S(2)}) async-start(f32[4,8,896]{2,1,0:T(8,128)} %bitcast.3), calls=%async_computation.1 | async-start | bytes 229376 | tf_op jit(solution)/shard_map/all_to_all | solution.py:148
  21.1 17.3 %collective-permute-start = (f32[64,448]{1,0:T(8,128)S(1)}, f32[64,448]{1,0:T(8,128)S(1)}, u32[]{:S(2)}, u32[]{:S(2)}) collective-permute-start(f32[64,448]{1,0:T(8,128)S(1)} %bitcast.41), channel_id=1, source_target_pairs={{0,0},{1,1},{2,2},{3,3},{4,128},{5,129},{6,130},{7,131},{8,256},{9... | collective-permute-start | bytes 344072 | tf_op jit(solution)/shard_map/ppermute | solution.py:144
  38.4 32.7 %collective-permute-start.2 = (f32[64,448]{1,0:T(8,128)S(1)}, f32[64,448]{1,0:T(8,128)S(1)}, u32[]{:S(2)}, u32[]{:S(2)}) collective-permute-start(f32[64,448]{1,0:T(8,128)S(1)} %collective-permute-done), channel_id=1, source_target_pairs={{0,0},{1,32},{2,64},{3,96},{128,128},{129,160},{130,192},{131,224}... | collective-permute-start | bytes 344072 | tf_op jit(solution)/shard_map/ppermute | solution.py:119
  48.0 23.1 %collective-permute-start.1 = (f32[64,448]{1,0:T(8,128)S(1)}, f32[64,448]{1,0:T(8,128)S(1)}, u32[]{:S(2)}, u32[]{:S(2)}) collective-permute-start(f32[64,448]{1,0:T(8,128)S(1)} %collective-permute-done), channel_id=1, source_target_pairs={{0,16},{1,48},{2,80},{3,112},{128,144},{129,176},{130,208},{131,24... | collective-permute-start | bytes 344072 | tf_op jit(solution)/shard_map/ppermute | solution.py:119
  67.6 7.3 %all-to-all-start.2 = ((f32[2,32,896]{2,1,0:T(8,128)}), f32[2,32,896]{2,1,0:T(8,128)S(1)}, u32[]{:S(2)}, u32[]{:S(2)}) async-start(f32[2,32,896]{2,1,0:T(8,128)} %pad_maximum_fusion.1), calls=%async_computation.2 | async-start | bytes 458752 | tf_op jit(solution)/shard_map/all_to_all | solution.py:154
  110.8 2.7 %copy-start.3 = (f32[64,448]{1,0:T(8,128)}, f32[64,448]{1,0:T(8,128)S(1)}, u32[]{:S(2)}) copy-start(f32[64,448]{1,0:T(8,128)S(1)} %fusion.3) | copy-start | bytes 344068
